TPU v7x, 256 devices: a whole 4x4x8 slice. The times are simulated.
256 devices in a mesh: term: 8 (over y, x_hi), sector: 32 (over x_lo, z, core).
Axes of the slice: x: 4 (x_hi: 2, x_lo: 2; x = x_hi * 2 + x_lo), y: 4, z: 8, core: 2. Of those that a mesh axis runs over, the one named last changes fastest.
Arguments:
- psi: float32 [512, 128, 128], P('sector'), may hold values from -6 to 6
- left_env: float32 [32, 512, 128, 128], P('term', 'sector'), may hold values from -0.5 to 0.5
- right_env: float32 [32, 512, 128, 128], P('term', 'sector'), may hold values from -0.09375 to 0.09375
- target: int32 [32, 512], P('term', 'sector'), may hold values from 0 to 511, as said below
Outputs:
- sigma: float32 [512, 128, 128], P('sector', 'term')
Inputs may be any that keep to these rules, and one draw needn't show every extreme that they name: Among the 4 * 16 pairs of terms w in one block of 4 consecutive terms and source blocks s in one block of 16 consecutive blocks, at most 4 have their target in any one block of 16 consecutive target blocks, and exactly 4 do for some such block.
All inputs are finite; a program needn't handle non-finite values.
Results may differ from a plain program's by a relative error of at most 0.0001.
Values sent between devices are 32-bit elements; how exact they have to be, the bound alone decides.
No kernel may reach another device: no remote copies, remote signals or barrier semaphores. Data moves between devices by JAX's collectives and lax.ppermute only.
A program may use at most 128 MiB of HBM per device.

v0:
```python
import jax
import jax.numpy as jnp
from jax import lax
from jax.sharding import PartitionSpec as P

CAP = 4


def route_terms(contracted, target_part, right_part, exchanger):
    term_count, sector_count, block_width, unused = contracted.shape
    item_count = term_count * sector_count
    slot_count = lax.axis_size("sector") * CAP
    flat_target = target_part.reshape(item_count)
    owner_dev = flat_target // sector_count
    local_target = flat_target % sector_count
    item_index = jnp.arange(item_count, dtype=jnp.int32)
    term_index = item_index // sector_count
    earlier = (owner_dev[:, None] == owner_dev[None, :]) & (
        item_index[None, :] < item_index[:, None]
    )
    rank_slot = jnp.sum(earlier.astype(jnp.int32), axis=1)
    slot_index = owner_dev * CAP + rank_slot
    outgoing = jnp.zeros((slot_count, block_width, block_width), jnp.float32)
    outgoing = outgoing.at[slot_index].set(contracted.reshape(item_count, block_width, block_width))
    labels = (
        jnp.zeros((slot_count,), jnp.int32)
        .at[slot_index]
        .set(term_index * sector_count + local_target + 1)
    )
    incoming, labels_in = exchanger(outgoing, labels)
    occupied = labels_in > 0
    pair_index = jnp.maximum(labels_in - 1, 0)
    target_in = pair_index % sector_count
    right_blocks = right_part.reshape(item_count, block_width, block_width)[pair_index]
    products = jnp.einsum("nab,nbc->nac", incoming, right_blocks, precision=lax.Precision.HIGHEST)
    selector = (
        (target_in[None, :] == jnp.arange(sector_count)[:, None]) & occupied[None, :]
    ).astype(jnp.float32)
    partial_value = jnp.dot(
        selector,
        products.reshape(slot_count, block_width * block_width),
        precision=lax.Precision.HIGHEST,
    )
    partial_value = partial_value.reshape(sector_count, block_width, block_width)
    return partial_value


def on_device(psi, left_env, right_env, target):

    def relay_all(outgoing, labels):
        return (
            lax.all_to_all(outgoing, "sector", split_axis=0, concat_axis=0, tiled=True),
            lax.all_to_all(labels, "sector", split_axis=0, concat_axis=0, tiled=True),
        )

    contracted = jnp.einsum("wsab,sbc->wsac", left_env, psi, precision=lax.Precision.HIGHEST)
    partial_value = route_terms(contracted, target, right_env, relay_all)
    return lax.psum_scatter(partial_value, "term", scatter_dimension=1, tiled=True)


def solution(mesh):
    in_specs = (
        P("sector", None, None),
        P("term", "sector", None, None),
        P("term", "sector", None, None),
        P("term", "sector"),
    )
    out_specs = P("sector", "term", None)
    return jax.shard_map(
        on_device, mesh=mesh, in_specs=in_specs, out_specs=out_specs, check_vma=False
    )
```

profile of v0, /device:TPU:96, one launch (start us, length us, event | category | flops | bytes accessed | tf_op | source)
XLA Modules:
  0.0 369.1 jit_solution(3594806636337813760)
XLA Ops:
  6.5 0.0 copy-start
  6.5 0.9 reshape.187
  7.4 0.8 reshape.186
  8.2 0.2 convert_reduce_fusion
  8.4 0.8 scatter_custom_fusion
  9.1 0.7 all_to_all.9
  9.9 8.7 %all-to-all-start = ((s32[32,4,1]{1,2,0:T(1,128)}), s32[32,4,1]{1,2,0:T(1,128)S(1)}, u32[]{:S(2)}, u32[]{:S(2)}) async-start(s32[32,4,1]{1,2,0:T(1,128)} %bitcast.2), calls=%async_computation | async-start | bytes 32768 | tf_op jit(solution)/shard_map/all_to_all | solution.py:53
  18.6 0.0 copy-done
  18.6 7.9 %fusion.2 = f32[4,16,128,128]{2,3,0,1:T(8,128)} fusion(f32[4,16,128,128]{3,2,1,0:T(8,128)} %param.5, f32[16,128,128]{2,1,0:T(8,128)S(1)} %copy-done), kind=kOutput, calls=%fused_computation.6 | convolution fusion | flops 1610612736 | bytes 9437184 | tf_op jit(solution)/shard_map/wsab,sbc->wsac/dot_general | solution.py:56
  26.6 5.4 %copy.23 = f32[4,16,128,128]{3,2,1,0:T(8,128)} copy(f32[4,16,128,128]{2,3,0,1:T(8,128)} %fusion.2) | data formatting | bytes 8388608 | tf_op jit(solution)/shard_map/wsab,sbc->wsac/transpose | solution.py:56
  31.9 4.3 %broadcast_in_dim.2 = f32[128,128,128]{2,1,0:T(8,128)} broadcast(f32[]{:T(128)} %constant.59.clone.1), dimensions={} | broadcast | bytes 8388612 | tf_op jit(solution)/shard_map/broadcast_in_dim | solution.py:23
  36.2 12.0 %scatter_fusion = f32[128,128,128]{2,1,0:T(8,128)} fusion(f32[128,128,128]{2,1,0:T(8,128)} %broadcast_in_dim.2, s32[64]{0:T(128)S(1)} %fusion.17, f32[64,128,128]{2,1,0:T(8,128)} %bitcast.34), kind=kCustom, calls=%fused_computation.2 | custom fusion | bytes 12583168 | tf_op jit(solution)/shard_map/scatter | solution.py:24
  48.1 0.0 all-to-all-done
  48.1 8.3 %all-to-all-start.1 = ((f32[128,128,128]{2,1,0:T(8,128)}), f32[128,128,128]{2,1,0:T(8,128)}, u32[]{:S(2)}, u32[]{:S(2)}) async-start(f32[128,128,128]{2,1,0:T(8,128)} %scatter_fusion), calls=%async_computation.1 | async-start | bytes 16777216 | tf_op jit(solution)/shard_map/all_to_all | solution.py:52
  56.4 0.2 reduce-scatter.2.cloned.1.call-start
  56.7 0.1 and_reduce_fusion
  56.8 0.1 reshape.193
  56.9 0.1 rem.73
  57.0 0.1 compare_reduce_fusion
  57.0 0.1 gt.11
  57.2 6.5 %gather_fusion = f32[128,128,128]{2,1,0:T(8,128)} fusion(f32[64,128,128]{2,1,0:T(8,128)} %bitcast.33, s32[1024]{0:T(1024)S(1)} %pad_clamp_fusion), kind=kCustom, calls=%fused_computation | custom fusion | bytes 16777728 | tf_op jit(solution)/shard_map/gather | solution.py:34
  63.7 180.8 %all-to-all-done.1 = f32[128,128,128]{2,1,0:T(8,128)} async-done(((f32[128,128,128]{2,1,0:T(8,128)}), f32[128,128,128]{2,1,0:T(8,128)}, u32[]{:S(2)}, u32[]{:S(2)}) %all-to-all-start.1) | async-done | bytes 8388640 | tf_op jit(solution)/shard_map/all_to_all | solution.py:52
  244.4 12.2 %fusion.20 = f32[128,128,128]{2,1,0:T(8,128)S(1)} fusion(f32[128,128,128]{2,1,0:T(8,128)} %all-to-all-done.1, f32[128,128,128]{2,1,0:T(8,128)} %gather_fusion), kind=kOutput, calls=%fused_computation.44 | convolution fusion | flops 3221225472 | bytes 25165824 | tf_op jit(solution)/shard_map/nab,nbc->nac/dot_general | solution.py:35
  256.7 9.7 %copy.35 = f32[16,8,128,128]{3,1,2,0:T(8,128)} copy(f32[16,8,128,128]{3,2,1,0:T(8,128)S(1)} %bitcast.30) | data formatting | bytes 16777216
  266.4 0.0 copy-start.1
  266.4 9.1 %copy.24 = f32[16384,128]{1,0:T(8,128)} copy(f32[16384,128]{0,1:T(8,128)} %bitcast.32) | data formatting | bytes 16777216 | tf_op jit(solution)/shard_map/dot_general | solution.py:39
  275.5 8.3 %fusion.9 = f32[16,128,128]{2,0,1:T(8,128)} fusion(f32[128,128,128]{2,1,0:T(8,128)} %bitcast.31, s32[128]{0:T(128)S(1)} %and_select_fusion, pred[128]{0:T(512)(128)(4,1)S(1)} %gt.11), kind=kOutput, calls=%fused_computation.17 | convolution fusion | flops 402657280 | bytes 9437824 | tf_op jit(solution)/shard_map/dot_general | solution.py:39
  283.8 0.0 reduce-scatter.2.cloned.1.call-update
  283.9 76.8 %reduce-scatter.2.cloned.1.call-done = f32[16,16,128]{2,0,1:T(8,128)} async-done(((f32[16,128,128]{2,0,1:T(8,128)}), f32[16,16,128]{2,0,1:T(8,128)}) %reduce-scatter.2.cloned.1.call-update) | async-done | bytes 131088 | tf_op jit(solution)/shard_map/reduce_scatter | solution.py:58
  360.7 1.6 copy.25
  362.3 0.0 copy-done.1
  (4 shorter events, 0.0 us)
Async XLA Ops:
  6.5 12.1 %copy-start = (f32[16,128,128]{2,1,0:T(8,128)S(1)}, f32[16,128,128]{2,1,0:T(8,128)}, u32[]{:S(2)}) copy-start(f32[16,128,128]{2,1,0:T(8,128)} %param.4) | copy-start | bytes 3145732
  9.9 38.3 %all-to-all-start = ((s32[32,4,1]{1,2,0:T(1,128)}), s32[32,4,1]{1,2,0:T(1,128)S(1)}, u32[]{:S(2)}, u32[]{:S(2)}) async-start(s32[32,4,1]{1,2,0:T(1,128)} %bitcast.2), calls=%async_computation | async-start | bytes 32768 | tf_op jit(solution)/shard_map/all_to_all | solution.py:53
  48.1 196.3 %all-to-all-start.1 = ((f32[128,128,128]{2,1,0:T(8,128)}), f32[128,128,128]{2,1,0:T(8,128)}, u32[]{:S(2)}, u32[]{:S(2)}) async-start(f32[128,128,128]{2,1,0:T(8,128)} %scatter_fusion), calls=%async_computation.1 | async-start | bytes 16777216 | tf_op jit(solution)/shard_map/all_to_all | solution.py:52
  56.4 304.2 %reduce-scatter.2.cloned.1.call-start = ((), (), s32[]{:S(2)}) async-start(), calls=%async_computation.3 | async-start | bytes 1179648 | tf_op jit(solution)/shard_map/reduce_scatter | solution.py:58
  266.4 95.8 %copy-start.1 = (f32[16,128,128]{2,1,0:T(8,128)S(1)}, f32[16,128,128]{2,1,0:T(8,128)}, u32[]{:S(2)}) copy-start(f32[16,128,128]{2,1,0:T(8,128)} %param.4) | copy-start | bytes 3145732
Sparse Core Ops, SparseCore 0:
  284.0 76.6 reduce-scatter.1
where the time goes:
time: 370 us; the launch traced here: 369 us
  waiting for transfers between devices  258 us (70%)
  local copies, waits for them, and re-layouts  51.9 us (14%)
  matrix products  28.5 us (8%)
  starting transfers between devices  17.3 us (5%)
  between operations  13.5 us (4%)
    all_to_all x1, waiting for transfers between devices, relay_all(): lax.all_to_all(outgoing, 'sector', split_axis=0, concat_axis=0, tiled=True)  181 us
    reduce_scatter x1, waiting for transfers between devices, on_device(): lax.psum_scatter(partial_value, 'term', scatter_dimension=1, tiled=True)  76.8 us
    dot_general x1, matrix products, route_terms(): jnp.einsum('nab,nbc->nac', incoming, right_blocks, precision=lax.Precisio...  12.2 us
    scatter x1, local copies, waits for them, and re-layouts, route_terms(): outgoing.at[slot_index]  12 us
    unnamed x5, local copies, waits for them, and re-layouts  9.76 us
    dot_general x1, local copies, waits for them, and re-layouts, route_terms(): jnp.dot(selector, products.reshape(slot_count, block_width * block_width)...  9.08 us
    all_to_all x1, starting transfers between devices, relay_all(): lax.all_to_all(labels, 'sector', split_axis=0, concat_axis=0, tiled=True)  8.75 us
    dot_general x1, matrix products, route_terms(): jnp.dot(selector, products.reshape(slot_count, block_width * block_width)...  8.34 us
  transfers between devices with their start and end apart: 3, of which 2 were waited for; matrix products, arithmetic and copies ran while one was open for 10% of the time, Pallas kernels for 0%

commit v1 on v0

v1 whole, which is shorter than its diff:
```python
import jax
import jax.numpy as jnp
from jax import lax
from jax.experimental import pallas as pl
from jax.experimental.pallas import tpu as pltpu
from jax.sharding import PartitionSpec as P

CAP = 4
GROUP = 8


def slot_tables(target_part):
    term_count, sector_count = target_part.shape
    item_count = term_count * sector_count
    slot_count = lax.axis_size("sector") * CAP
    flat_target = target_part.reshape(item_count)
    owner_dev = flat_target // sector_count
    local_target = flat_target % sector_count
    item_index = jnp.arange(item_count, dtype=jnp.int32)
    term_index = item_index // sector_count
    earlier = (owner_dev[:, None] == owner_dev[None, :]) & (
        item_index[None, :] < item_index[:, None]
    )
    rank_slot = jnp.sum(earlier.astype(jnp.int32), axis=1)
    slot_index = owner_dev * CAP + rank_slot
    match = slot_index[None, :] == jnp.arange(slot_count, dtype=jnp.int32)[:, None]
    occupied = jnp.any(match, axis=1)
    item_of_slot = jnp.sum(jnp.where(match, item_index[None, :], 0), axis=1)
    label_of_item = term_index * sector_count + local_target + 1
    labels = jnp.where(occupied, label_of_item[item_of_slot], 0).astype(jnp.int32)
    return item_of_slot.astype(jnp.int32), labels


def sender_kernel(item_ref, label_ref, left_ref, psi_ref, out_ref):
    sector_count = psi_ref.shape[0]
    step = pl.program_id(0)
    for j in range(GROUP):
        slot = step * GROUP + j
        item = item_ref[slot]
        term = item // sector_count
        source = item % sector_count

        @pl.when(label_ref[slot] > 0)
        def _():
            out_ref[j] = jnp.dot(
                left_ref[term, source],
                psi_ref[source],
                precision=lax.Precision.HIGHEST,
                preferred_element_type=jnp.float32,
            )

        @pl.when(label_ref[slot] == 0)
        def _():
            out_ref[j] = jnp.zeros(out_ref.shape[1:], jnp.float32)


def send_blocks(item_of_slot, labels, left_env, psi):
    slot_count = item_of_slot.shape[0]
    width = psi.shape[-1]
    grid_spec = pltpu.PrefetchScalarGridSpec(
        num_scalar_prefetch=2,
        grid=(slot_count // GROUP,),
        in_specs=[
            pl.BlockSpec(left_env.shape, lambda g, *_: (0, 0, 0, 0)),
            pl.BlockSpec(psi.shape, lambda g, *_: (0, 0, 0)),
        ],
        out_specs=pl.BlockSpec((GROUP, width, width), lambda g, *_: (g, 0, 0)),
    )
    return pl.pallas_call(
        sender_kernel,
        grid_spec=grid_spec,
        out_shape=jax.ShapeDtypeStruct((slot_count, width, width), jnp.float32),
        compiler_params=pltpu.CompilerParams(vmem_limit_bytes=48 * 1024 * 1024),
    )(item_of_slot, labels, left_env, psi)


def receiver_kernel(label_ref, incoming_ref, right_ref, out_ref):
    sector_count = out_ref.shape[0]
    step = pl.program_id(0)

    @pl.when(step == 0)
    def _():
        out_ref[...] = jnp.zeros(out_ref.shape, jnp.float32)

    for j in range(GROUP):
        label = label_ref[step * GROUP + j]

        @pl.when(label > 0)
        def _():
            pair = label - 1
            term = pair // sector_count
            tgt = pair % sector_count
            out_ref[tgt] += jnp.dot(
                incoming_ref[j],
                right_ref[term, tgt],
                precision=lax.Precision.HIGHEST,
                preferred_element_type=jnp.float32,
            )


def receive_blocks(labels, incoming, right_env):
    slot_count = labels.shape[0]
    sector_count = right_env.shape[1]
    width = right_env.shape[-1]
    grid_spec = pltpu.PrefetchScalarGridSpec(
        num_scalar_prefetch=1,
        grid=(slot_count // GROUP,),
        in_specs=[
            pl.BlockSpec((GROUP, width, width), lambda g, *_: (g, 0, 0)),
            pl.BlockSpec(right_env.shape, lambda g, *_: (0, 0, 0, 0)),
        ],
        out_specs=pl.BlockSpec((sector_count, width, width), lambda g, *_: (0, 0, 0)),
    )
    return pl.pallas_call(
        receiver_kernel,
        grid_spec=grid_spec,
        out_shape=jax.ShapeDtypeStruct((sector_count, width, width), jnp.float32),
        compiler_params=pltpu.CompilerParams(vmem_limit_bytes=48 * 1024 * 1024),
    )(labels, incoming, right_env)


def on_device(psi, left_env, right_env, target):
    item_of_slot, labels = slot_tables(target)
    labels_in = lax.all_to_all(labels, "sector", split_axis=0, concat_axis=0, tiled=True)
    outgoing = send_blocks(item_of_slot, labels, left_env, psi)
    incoming = lax.all_to_all(outgoing, "sector", split_axis=0, concat_axis=0, tiled=True)
    partial_value = receive_blocks(labels_in, incoming, right_env)
    term_count = lax.axis_size("term")
    sector_count, width, unused = partial_value.shape
    rows = width // term_count
    pieces = partial_value.reshape(sector_count, term_count, rows, width).transpose(1, 0, 2, 3)
    gathered = lax.all_to_all(pieces, "term", split_axis=0, concat_axis=0, tiled=True)
    return jnp.sum(gathered, axis=0)


def solution(mesh):
    in_specs = (
        P("sector", None, None),
        P("term", "sector", None, None),
        P("term", "sector", None, None),
        P("term", "sector"),
    )
    out_specs = P("sector", "term", None)
    return jax.shard_map(
        on_device, mesh=mesh, in_specs=in_specs, out_specs=out_specs, check_vma=False
    )
```

time: 370 us -> 275 us (0.74)
  waiting for transfers between devices: 258 us -> 187 us
  local copies, waits for them, and re-layouts: 51.9 us -> 9 us
  Pallas kernels: 0 us -> 36.6 us
  matrix products: 28.5 us -> 0 us
  blocking collectives: 0 us -> 22.8 us
  between operations: 13.5 us -> 0.1 us
    reduce_scatter x1 -> x0, waiting for transfers between devices: 76.8 us -> none  [on_device(): lax.psum_scatter(partial_value, 'term', scatter_dimension=1, tiled=True)]
    pallas_call x0 -> x2, Pallas kernels: none -> 36.6 us  [the longest x1 19.4 us: receive_blocks(): pl.pallas_call(receiver_kernel, grid_spec=grid_spec, out_shape=jax.ShapeD...]
    dot_general x3 -> x0, matrix products: 28.5 us -> none  [the longest x1 12.2 us: route_terms(): jnp.einsum('nab,nbc->nac', incoming, right_blocks, precision=lax.Precisio...]
    all_to_all x0 -> x1, blocking collectives: none -> 22.8 us  [on_device(): lax.all_to_all(pieces, 'term', split_axis=0, concat_axis=0, tiled=True)]
    scatter x2 -> x0, local copies, waits for them, and re-layouts: 12.7 us -> none  [the longest x1 12 us: route_terms(): outgoing.at[slot_index]]
    dot_general x1 -> x0, local copies, waits for them, and re-layouts: 9.08 us -> none  [route_terms(): jnp.dot(selector, products.reshape(slot_count, block_width * block_width)...]
    all_to_all x2, waiting for transfers between devices: 181 us -> 187 us  [the longest x1 187 us: on_device(): lax.all_to_all(outgoing, 'sector', split_axis=0, concat_axis=0, tiled=True)]
    transpose x1 -> x0, local copies, waits for them, and re-layouts: 5.35 us -> none  [on_device(): jnp.einsum('wsab,sbc->wsac', left_env, psi, precision=lax.Precision.HIGHEST)]
  transfers between devices with their start and end apart: 3 -> 2, of which waited for: 2 -> 1; matrix products, arithmetic and copies ran while one was open for 10% -> 0% of each run, Pallas kernels for 0% -> 6%
where the time goes in v1:
time: 275 us; the launch traced here: 274 us
  waiting for transfers between devices  187 us (68%)
  Pallas kernels  36.6 us (13%)
  blocking collectives  22.8 us (8%)
  starting transfers between devices  17.2 us (6%)
  local copies, waits for them, and re-layouts  9 us (3%)
    all_to_all x1, waiting for transfers between devices, on_device(): lax.all_to_all(outgoing, 'sector', split_axis=0, concat_axis=0, tiled=True)  187 us
    all_to_all x1, blocking collectives, on_device(): lax.all_to_all(pieces, 'term', split_axis=0, concat_axis=0, tiled=True)  22.8 us
    pallas_call x1, Pallas kernels, receive_blocks(): pl.pallas_call(receiver_kernel, grid_spec=grid_spec, out_shape=jax.ShapeD...  19.4 us
    pallas_call x1, Pallas kernels, send_blocks(): pl.pallas_call(sender_kernel, grid_spec=grid_spec, out_shape=jax.ShapeDty...  17.3 us
    all_to_all x1, starting transfers between devices, on_device(): lax.all_to_all(labels, 'sector', split_axis=0, concat_axis=0, tiled=True)  8.75 us
    all_to_all x1, starting transfers between devices, on_device(): lax.all_to_all(outgoing, 'sector', split_axis=0, concat_axis=0, tiled=True)  8.49 us
    unnamed x6, local copies, waits for them, and re-layouts  5.6 us
  transfers between devices with their start and end apart: 2, of which 1 were waited for; matrix products, arithmetic and copies ran while one was open for 0% of the time, Pallas kernels for 6%

profile of v1, /device:TPU:96, one launch (start us, length us, event | category | flops | bytes accessed | tf_op | source)
XLA Modules:
  0.0 274.3 jit_solution(14338539191954529989)
XLA Ops:
  0.0 0.8 reshape.109
  0.8 0.2 convert_reduce_fusion
  1.0 0.1 select_reduce_fusion.item_ref
  1.1 0.1 fusion
  1.2 1.2 gather_fusion
  2.4 0.7 select_n.52
  3.1 8.7 %all-to-all-start = ((s32[32,4,1]{1,2,0:T(1,128)}), s32[32,4,1]{1,2,0:T(1,128)S(1)}, u32[]{:S(2)}, u32[]{:S(2)}) async-start(s32[32,4,1]{1,2,0:T(1,128)} %bitcast.2), calls=%async_computation | async-start | bytes 32768 | tf_op jit(solution)/shard_map/all_to_all | solution.py:124
  11.9 0.0 copy-start
  11.9 2.2 copy-done
  14.1 0.0 copy-start.2
  14.1 1.2 copy-done.2
  15.3 17.3 %shard_map.46 = f32[128,128,128]{2,1,0:T(8,128)} custom-call(s32[128]{0:T(128)S(1)} %select_reduce_fusion.item_ref, s32[128]{0:T(128)S(1)} %broadcast_select_fusion.label_ref, f32[4,16,128,128]{3,2,1,0:T(8,128)S(1)} %copy-done, f32[16,128,128]{2,1,0:T(8,128)S(1)} %copy-done.2), custom_call_target="tpu_custom_call" | custom-call | tf_op jit(solution)/shard_map/pallas_call | solution.py:69
  32.6 0.0 all-to-all-done
  32.6 8.5 %all-to-all-start.1 = ((f32[128,128,128]{2,1,0:T(8,128)}), f32[128,128,128]{2,1,0:T(8,128)}, u32[]{:S(2)}, u32[]{:S(2)}) async-start(f32[128,128,128]{2,1,0:T(8,128)} %shard_map.46), calls=%async_computation.1 | async-start | bytes 16777216 | tf_op jit(solution)/shard_map/all_to_all | solution.py:126
  41.1 0.5 broadcast.139
  41.6 0.7 reduce.3
  42.3 0.1 all_to_all.12.label_ref
  42.4 186.7 %all-to-all-done.1.incoming_ref = f32[128,128,128]{2,1,0:T(8,128)} async-done(((f32[128,128,128]{2,1,0:T(8,128)}), f32[128,128,128]{2,1,0:T(8,128)}, u32[]{:S(2)}, u32[]{:S(2)}) %all-to-all-start.1) | async-done | bytes 8388640 | tf_op jit(solution)/shard_map/all_to_all | solution.py:126
  229.1 0.0 copy-start.1
  229.1 2.2 copy-done.1
  231.3 19.4 %shard_map.47 = f32[16,128,128]{2,1,0:T(8,128)S(1)} custom-call(s32[128]{0:T(128)S(1)} %all_to_all.12.label_ref, f32[128,128,128]{2,1,0:T(8,128)} %all-to-all-done.1.incoming_ref, f32[4,16,128,128]{3,2,1,0:T(8,128)S(1)} %copy-done.1), custom_call_target="tpu_custom_call" | custom-call | tf_op jit(solution)/shard_map/pallas_call | solution.py:114
  250.7 0.1 copy.10
  250.8 22.8 %all_to_all.18 = f32[8,16,16,128]{3,2,1,0:T(8,128)S(1)} all-to-all(f32[8,16,16,128]{3,2,1,0:T(8,128)S(1)} %bitcast.11), channel_id=1, replica_groups=mesh['term'=8,'sector'=32] {'term'}, dimensions={0} | all-to-all | bytes 2097152 | tf_op jit(solution)/shard_map/all_to_all | solution.py:132
  273.5 0.7 reduce_sum.32
  (5 shorter events, 0.0 us)
Async XLA Ops:
  3.1 29.4 %all-to-all-start = ((s32[32,4,1]{1,2,0:T(1,128)}), s32[32,4,1]{1,2,0:T(1,128)S(1)}, u32[]{:S(2)}, u32[]{:S(2)}) async-start(s32[32,4,1]{1,2,0:T(1,128)} %bitcast.2), calls=%async_computation | async-start | bytes 32768 | tf_op jit(solution)/shard_map/all_to_all | solution.py:124
  11.9 2.2 copy-start
  14.1 1.2 copy-start.2
  32.6 196.5 %all-to-all-start.1 = ((f32[128,128,128]{2,1,0:T(8,128)}), f32[128,128,128]{2,1,0:T(8,128)}, u32[]{:S(2)}, u32[]{:S(2)}) async-start(f32[128,128,128]{2,1,0:T(8,128)} %shard_map.46), calls=%async_computation.1 | async-start | bytes 16777216 | tf_op jit(solution)/shard_map/all_to_all | solution.py:126
  229.1 2.2 copy-start.1

commit v2 on v1

--- a/solution.py
+++ b/solution.py
@@ -7,6 +7,18 @@
 
 CAP = 4
 GROUP = 8
+
+
+def split_dot(a, b):
+    a_hi = a.astype(jnp.bfloat16)
+    a_lo = (a - a_hi.astype(jnp.float32)).astype(jnp.bfloat16)
+    b_hi = b.astype(jnp.bfloat16)
+    b_lo = (b - b_hi.astype(jnp.float32)).astype(jnp.bfloat16)
+
+    def part(x, y):
+        return jnp.dot(x, y, preferred_element_type=jnp.float32)
+
+    return part(a_hi, b_hi) + (part(a_hi, b_lo) + part(a_lo, b_hi))
 
 
 def slot_tables(target_part):
@@ -42,12 +54,7 @@
 
         @pl.when(label_ref[slot] > 0)
         def _():
-            out_ref[j] = jnp.dot(
-                left_ref[term, source],
-                psi_ref[source],
-                precision=lax.Precision.HIGHEST,
-                preferred_element_type=jnp.float32,
-            )
+            out_ref[j] = split_dot(left_ref[term, source], psi_ref[source])
 
         @pl.when(label_ref[slot] == 0)
         def _():
@@ -90,12 +97,7 @@
             pair = label - 1
             term = pair // sector_count
             tgt = pair % sector_count
-            out_ref[tgt] += jnp.dot(
-                incoming_ref[j],
-                right_ref[term, tgt],
-                precision=lax.Precision.HIGHEST,
-                preferred_element_type=jnp.float32,
-            )
+            out_ref[tgt] += split_dot(incoming_ref[j], right_ref[term, tgt])
 
 
 def receive_blocks(labels, incoming, right_env):

time: 275 us -> 271 us (0.985)
  Pallas kernels: 36.6 us -> 33.6 us
where the time goes in v2:
time: 271 us
  waiting for transfers between devices  187 us (69%)
  Pallas kernels  33.6 us (12%)
  blocking collectives  22.3 us (8%)
  starting transfers between devices  17.3 us (6%)
  local copies, waits for them, and re-layouts  9 us (3%)
    all_to_all x1, waiting for transfers between devices, on_device(): lax.all_to_all(outgoing, 'sector', split_axis=0, concat_axis=0, tiled=True)  187 us
    all_to_all x1, blocking collectives, on_device(): lax.all_to_all(pieces, 'term', split_axis=0, concat_axis=0, tiled=True)  22.3 us
    pallas_call x1, Pallas kernels, receive_blocks(): pl.pallas_call(receiver_kernel, grid_spec=grid_spec, out_shape=jax.ShapeD...  18.3 us
    pallas_call x1, Pallas kernels, send_blocks(): pl.pallas_call(sender_kernel, grid_spec=grid_spec, out_shape=jax.ShapeDty...  15.4 us
    all_to_all x1, starting transfers between devices, on_device(): lax.all_to_all(labels, 'sector', split_axis=0, concat_axis=0, tiled=True)  8.75 us
    all_to_all x1, starting transfers between devices, on_device(): lax.all_to_all(outgoing, 'sector', split_axis=0, concat_axis=0, tiled=True)  8.57 us
    unnamed x6, local copies, waits for them, and re-layouts  5.6 us
  transfers between devices with their start and end apart: 2, of which 1 were waited for; matrix products, arithmetic and copies ran while one was open for 0% of the time, Pallas kernels for 6%

profile of v2, /device:TPU:96, one launch (start us, length us, event | category | flops | bytes accessed | tf_op | source)
XLA Modules:
  0.0 270.8 jit_solution(13907754911483111270)
XLA Ops:
  0.0 0.8 reshape.109
  0.8 0.2 convert_reduce_fusion
  1.0 0.1 select_reduce_fusion.item_ref
  1.1 0.1 fusion
  1.2 1.2 gather_fusion
  2.4 0.7 select_n.52
  3.1 8.7 %all-to-all-start = ((s32[32,4,1]{1,2,0:T(1,128)}), s32[32,4,1]{1,2,0:T(1,128)S(1)}, u32[]{:S(2)}, u32[]{:S(2)}) async-start(s32[32,4,1]{1,2,0:T(1,128)} %bitcast.2), calls=%async_computation | async-start | bytes 32768 | tf_op jit(solution)/shard_map/all_to_all | solution.py:126
  11.9 0.0 copy-start
  11.9 2.2 copy-done
  14.1 0.0 copy-start.2
  14.1 1.2 copy-done.2
  15.3 15.4 %shard_map.46 = f32[128,128,128]{2,1,0:T(8,128)} custom-call(s32[128]{0:T(128)S(1)} %select_reduce_fusion.item_ref, s32[128]{0:T(128)S(1)} %broadcast_select_fusion.label_ref, f32[4,16,128,128]{3,2,1,0:T(8,128)S(1)} %copy-done, f32[16,128,128]{2,1,0:T(8,128)S(1)} %copy-done.2), custom_call_target="tpu_custom_call" | custom-call | tf_op jit(solution)/shard_map/pallas_call | solution.py:76
  30.7 0.0 all-to-all-done
  30.7 8.6 %all-to-all-start.1 = ((f32[128,128,128]{2,1,0:T(8,128)}), f32[128,128,128]{2,1,0:T(8,128)}, u32[]{:S(2)}, u32[]{:S(2)}) async-start(f32[128,128,128]{2,1,0:T(8,128)} %shard_map.46), calls=%async_computation.1 | async-start | bytes 16777216 | tf_op jit(solution)/shard_map/all_to_all | solution.py:128
  39.3 0.5 broadcast.139
  39.8 0.7 reduce.3
  40.5 0.1 all_to_all.12.label_ref
  40.6 186.7 %all-to-all-done.1.incoming_ref = f32[128,128,128]{2,1,0:T(8,128)} async-done(((f32[128,128,128]{2,1,0:T(8,128)}), f32[128,128,128]{2,1,0:T(8,128)}, u32[]{:S(2)}, u32[]{:S(2)}) %all-to-all-start.1) | async-done | bytes 8388640 | tf_op jit(solution)/shard_map/all_to_all | solution.py:128
  227.3 0.0 copy-start.1
  227.3 2.2 copy-done.1
  229.5 18.3 %shard_map.47 = f32[16,128,128]{2,1,0:T(8,128)S(1)} custom-call(s32[128]{0:T(128)S(1)} %all_to_all.12.label_ref, f32[128,128,128]{2,1,0:T(8,128)} %all-to-all-done.1.incoming_ref, f32[4,16,128,128]{3,2,1,0:T(8,128)S(1)} %copy-done.1), custom_call_target="tpu_custom_call" | custom-call | tf_op jit(solution)/shard_map/pallas_call | solution.py:116
  247.7 0.1 copy.10
  247.8 22.3 %all_to_all.18 = f32[8,16,16,128]{3,2,1,0:T(8,128)S(1)} all-to-all(f32[8,16,16,128]{3,2,1,0:T(8,128)S(1)} %bitcast.11), channel_id=1, replica_groups=mesh['term'=8,'sector'=32] {'term'}, dimensions={0} | all-to-all | bytes 2097152 | tf_op jit(solution)/shard_map/all_to_all | solution.py:134
  270.1 0.7 reduce_sum.32
  (5 shorter events, 0.0 us)
Async XLA Ops:
  3.1 27.5 %all-to-all-start = ((s32[32,4,1]{1,2,0:T(1,128)}), s32[32,4,1]{1,2,0:T(1,128)S(1)}, u32[]{:S(2)}, u32[]{:S(2)}) async-start(s32[32,4,1]{1,2,0:T(1,128)} %bitcast.2), calls=%async_computation | async-start | bytes 32768 | tf_op jit(solution)/shard_map/all_to_all | solution.py:126
  11.9 2.2 copy-start
  14.1 1.2 copy-start.2
  30.7 196.6 %all-to-all-start.1 = ((f32[128,128,128]{2,1,0:T(8,128)}), f32[128,128,128]{2,1,0:T(8,128)}, u32[]{:S(2)}, u32[]{:S(2)}) async-start(f32[128,128,128]{2,1,0:T(8,128)} %shard_map.46), calls=%async_computation.1 | async-start | bytes 16777216 | tf_op jit(solution)/shard_map/all_to_all | solution.py:128
  227.3 2.2 copy-start.1

commit v3 on v2

v3 whole, which is shorter than its diff:
```python
import functools

import jax
import jax.numpy as jnp
from jax import lax
from jax.experimental import pallas as pl
from jax.experimental.pallas import tpu as pltpu
from jax.sharding import PartitionSpec as P

CAP = 4
GROUP = 16
SPLIT = 2


def split_dot(a, b):
    a_hi = a.astype(jnp.bfloat16)
    a_lo = (a - a_hi.astype(jnp.float32)).astype(jnp.bfloat16)
    b_hi = b.astype(jnp.bfloat16)
    b_lo = (b - b_hi.astype(jnp.float32)).astype(jnp.bfloat16)

    def part(x, y):
        return jnp.dot(x, y, preferred_element_type=jnp.float32)

    return part(a_hi, b_hi) + (part(a_hi, b_lo) + part(a_lo, b_hi))


def slot_tables(target_part):
    term_count, sector_count = target_part.shape
    item_count = term_count * sector_count
    slot_count = lax.axis_size("sector") * CAP
    flat_target = target_part.reshape(item_count)
    owner_dev = flat_target // sector_count
    local_target = flat_target % sector_count
    item_index = jnp.arange(item_count, dtype=jnp.int32)
    term_index = item_index // sector_count
    earlier = (owner_dev[:, None] == owner_dev[None, :]) & (
        item_index[None, :] < item_index[:, None]
    )
    rank_slot = jnp.sum(earlier.astype(jnp.int32), axis=1)
    slot_index = owner_dev * CAP + rank_slot
    match = slot_index[None, :] == jnp.arange(slot_count, dtype=jnp.int32)[:, None]
    occupied = jnp.any(match, axis=1)
    item_of_slot = jnp.sum(jnp.where(match, item_index[None, :], 0), axis=1)
    label_of_item = term_index * sector_count + local_target + 1
    labels = jnp.where(occupied, label_of_item[item_of_slot], 0).astype(jnp.int32)
    return item_of_slot.astype(jnp.int32), labels


def sender_kernel(item_ref, label_ref, left_ref, psi_ref, *out_refs, term_count):
    sector_count = psi_ref.shape[0]
    width = psi_ref.shape[-1]
    band = width // term_count
    piece = band // SPLIT
    step = pl.program_id(0)
    for j in range(GROUP):
        slot = step * GROUP + j
        item = item_ref[slot]
        term = item // sector_count
        source = item % sector_count
        value = split_dot(left_ref[term, source], psi_ref[source])
        value = jnp.where(label_ref[slot] > 0, value, 0.0)
        for h, out_ref in enumerate(out_refs):
            for i in range(term_count):
                out_ref[j, pl.ds(i * piece, piece), :] = value[
                    i * band + h * piece:i * band + (h + 1) * piece, :
                ]


def send_blocks(item_of_slot, labels, left_env, psi, term_count):
    slot_count = item_of_slot.shape[0]
    width = psi.shape[-1]
    half = width // SPLIT
    grid_spec = pltpu.PrefetchScalarGridSpec(
        num_scalar_prefetch=2,
        grid=(slot_count // GROUP,),
        in_specs=[
            pl.BlockSpec(left_env.shape, lambda g, *_: (0, 0, 0, 0)),
            pl.BlockSpec(psi.shape, lambda g, *_: (0, 0, 0)),
        ],
        out_specs=[
            pl.BlockSpec((GROUP, half, width), lambda g, *_: (g, 0, 0)) for _ in range(SPLIT)
        ],
    )
    return pl.pallas_call(
        functools.partial(sender_kernel, term_count=term_count),
        grid_spec=grid_spec,
        out_shape=[
            jax.ShapeDtypeStruct((slot_count, half, width), jnp.float32) for _ in range(SPLIT)
        ],
        compiler_params=pltpu.CompilerParams(vmem_limit_bytes=48 * 1024 * 1024),
    )(item_of_slot, labels, left_env, psi)


def receiver_kernel(label_ref, incoming_ref, right_ref, out_ref):
    sector_count = out_ref.shape[0]
    step = pl.program_id(0)

    @pl.when(step == 0)
    def _():
        out_ref[...] = jnp.zeros(out_ref.shape, jnp.float32)

    targets = []
    values = []
    for j in range(GROUP):
        pair = jnp.maximum(label_ref[step * GROUP + j] - 1, 0)
        term = pair // sector_count
        tgt = pair % sector_count
        targets.append(tgt)
        values.append(split_dot(incoming_ref[j], right_ref[term, tgt]))
    for tgt, value in zip(targets, values):
        out_ref[tgt] += value


def receive_blocks(labels, incoming, right_env):
    slot_count = labels.shape[0]
    sector_count = right_env.shape[1]
    rows, width = incoming.shape[1:]
    grid_spec = pltpu.PrefetchScalarGridSpec(
        num_scalar_prefetch=1,
        grid=(slot_count // GROUP,),
        in_specs=[
            pl.BlockSpec((GROUP, rows, width), lambda g, *_: (g, 0, 0)),
            pl.BlockSpec(right_env.shape, lambda g, *_: (0, 0, 0, 0)),
        ],
        out_specs=pl.BlockSpec((sector_count, rows, width), lambda g, *_: (0, 0, 0)),
    )
    return pl.pallas_call(
        receiver_kernel,
        grid_spec=grid_spec,
        out_shape=jax.ShapeDtypeStruct((sector_count, rows, width), jnp.float32),
        compiler_params=pltpu.CompilerParams(vmem_limit_bytes=48 * 1024 * 1024),
    )(labels, incoming, right_env)


def on_device(psi, left_env, right_env, target):
    term_count = lax.axis_size("term")
    item_of_slot, labels = slot_tables(target)
    labels_in = lax.all_to_all(labels, "sector", split_axis=0, concat_axis=0, tiled=True)
    outgoing = send_blocks(item_of_slot, labels, left_env, psi, term_count)
    results = []
    for piece_out in outgoing:
        incoming = lax.all_to_all(piece_out, "sector", split_axis=0, concat_axis=0, tiled=True)
        partial_value = receive_blocks(labels_in, incoming, right_env)
        sector_count, rows, width = partial_value.shape
        pieces = partial_value.reshape(sector_count, term_count, rows // term_count, width)
        pieces = pieces.transpose(1, 0, 2, 3)
        gathered = lax.all_to_all(pieces, "term", split_axis=0, concat_axis=0, tiled=True)
        results.append(jnp.sum(gathered, axis=0))
    return jnp.concatenate(results, axis=1)


def solution(mesh):
    in_specs = (
        P("sector", None, None),
        P("term", "sector", None, None),
        P("term", "sector", None, None),
        P("term", "sector"),
    )
    out_specs = P("sector", "term", None)
    return jax.shard_map(
        on_device, mesh=mesh, in_specs=in_specs, out_specs=out_specs, check_vma=False
    )
```

time: 271 us -> 265 us (0.978)
  waiting for transfers between devices: 187 us -> 96.3 us
  blocking collectives: 22.3 us -> 103 us
  starting transfers between devices: 17.3 us -> 27.6 us
  Pallas kernels: 33.6 us -> 25.2 us
    all_to_all x1 -> x3, waiting for transfers between devices: 187 us -> 96.3 us  [the longest x1 84.1 us: on_device(): lax.all_to_all(piece_out, 'sector', split_axis=0, concat_axis=0, tiled=True)]
    all_to_all x1, blocking collectives: 22.3 us -> 103 us  [on_device(): lax.all_to_all(piece_out, 'sector', split_axis=0, concat_axis=0, tiled=True)]
    all_to_all x1 -> x3, starting transfers between devices: 8.57 us -> 18.9 us  [the longest x2 12.4 us: on_device(): lax.all_to_all(pieces, 'term', split_axis=0, concat_axis=0, tiled=True)]
    pallas_call x1, Pallas kernels: 15.4 us -> 8.87 us  [send_blocks(): pl.pallas_call(functools.partial(sender_kernel, term_count=term_count), g...]
    pallas_call x1 -> x2, Pallas kernels: 18.3 us -> 16.3 us  [receive_blocks(): pl.pallas_call(receiver_kernel, grid_spec=grid_spec, out_shape=jax.ShapeD...]
  transfers between devices with their start and end apart: 2 -> 4, of which waited for: 1 -> 3; matrix products, arithmetic and copies ran while one was open for 0% -> 1% of each run, Pallas kernels for 6% -> 10%
where the time goes in v3:
time: 265 us; the launch traced here: 264 us
  blocking collectives  103 us (39%)
  waiting for transfers between devices  96.3 us (36%)
  starting transfers between devices  27.6 us (10%)
  Pallas kernels  25.2 us (10%)
  local copies, waits for them, and re-layouts  10.4 us (4%)
    all_to_all x1, blocking collectives, on_device(): lax.all_to_all(piece_out, 'sector', split_axis=0, concat_axis=0, tiled=True)  103 us
    all_to_all x1, waiting for transfers between devices, on_device(): lax.all_to_all(piece_out, 'sector', split_axis=0, concat_axis=0, tiled=True)  84.1 us
    pallas_call x2, Pallas kernels, receive_blocks(): pl.pallas_call(receiver_kernel, grid_spec=grid_spec, out_shape=jax.ShapeD...  16.3 us
    all_to_all x2, starting transfers between devices, on_device(): lax.all_to_all(pieces, 'term', split_axis=0, concat_axis=0, tiled=True)  12.4 us
    all_to_all x2, waiting for transfers between devices, on_device(): lax.all_to_all(pieces, 'term', split_axis=0, concat_axis=0, tiled=True)  12.2 us
    pallas_call x1, Pallas kernels, send_blocks(): pl.pallas_call(functools.partial(sender_kernel, term_count=term_count), g...  8.87 us
    all_to_all x1, starting transfers between devices, on_device(): lax.all_to_all(labels, 'sector', split_axis=0, concat_axis=0, tiled=True)  8.75 us
    all_to_all x1, starting transfers between devices, on_device(): lax.all_to_all(piece_out, 'sector', split_axis=0, concat_axis=0, tiled=True)  6.5 us
  transfers between devices with their start and end apart: 4, of which 3 were waited for; matrix products, arithmetic and copies ran while one was open for 1% of the time, Pallas kernels for 10%

profile of v3, /device:TPU:96, one launch (start us, length us, event | category | flops | bytes accessed | tf_op | source)
XLA Modules:
  0.0 263.9 jit_solution(3224661553668136738)
XLA Ops:
  0.0 0.8 reshape.112
  0.8 0.2 convert_reduce_fusion
  1.0 0.1 select_reduce_fusion.item_ref
  1.1 0.1 fusion
  1.2 1.2 gather_fusion
  2.4 0.7 select_n.52
  3.1 8.7 %all-to-all-start = ((s32[32,4,1]{1,2,0:T(1,128)}), s32[32,4,1]{1,2,0:T(1,128)S(1)}, u32[]{:S(2)}, u32[]{:S(2)}) async-start(s32[32,4,1]{1,2,0:T(1,128)} %bitcast.2), calls=%async_computation | async-start | bytes 32768 | tf_op jit(solution)/shard_map/all_to_all | solution.py:138
  11.9 0.0 copy-start.2
  11.9 1.2 copy-done.2
  13.1 8.9 %shard_map.46 = (f32[128,64,128]{2,1,0:T(8,128)S(1)}, f32[128,64,128]{2,1,0:T(8,128)}) custom-call(s32[128]{0:T(128)S(1)} %select_reduce_fusion.item_ref, s32[128]{0:T(128)S(1)} %broadcast_select_fusion.label_ref, f32[4,16,128,128]{3,2,1,0:T(8,128)} %left_ref.1, f32[16,128,128]{2,1,0:T(8,128)S(1)} %copy-done.2), custom_call_target="tpu_custom_call" | custom-call | tf_op jit(solution)/shard_map/pallas_call | solution.py:84
  22.0 0.0 copy-start.1
  22.0 2.0 copy-done.1
  24.0 0.0 all-to-all-done
  24.0 102.5 %all_to_all.28.incoming_ref = f32[128,64,128]{2,1,0:T(8,128)} all-to-all(f32[128,64,128]{2,1,0:T(8,128)} %copy-done.1), channel_id=1, replica_groups=mesh['term'=8,'sector'=32] {'sector'}, dimensions={0} | all-to-all | bytes 8388608 | tf_op jit(solution)/shard_map/all_to_all | solution.py:142
  126.5 6.5 %all-to-all-start.3 = ((f32[128,64,128]{2,1,0:T(8,128)}), f32[128,64,128]{2,1,0:T(8,128)}, u32[]{:S(2)}, u32[]{:S(2)}) async-start(f32[128,64,128]{2,1,0:T(8,128)} %get-tuple-element.8), calls=%async_computation.3 | async-start | bytes 8388608 | tf_op jit(solution)/shard_map/all_to_all | solution.py:142
  133.0 0.5 broadcast.139
  133.5 0.7 reduce.3
  134.2 0.1 all_to_all.18.label_ref
  134.3 0.0 copy-start
  134.3 2.2 copy-done
  136.5 7.3 %shard_map.47 = f32[16,64,128]{2,1,0:T(8,128)S(1)} custom-call(s32[128]{0:T(128)S(1)} %all_to_all.18.label_ref, f32[128,64,128]{2,1,0:T(8,128)S(1)} %copy-done, f32[4,16,128,128]{3,2,1,0:T(8,128)} %right_ref.3), custom_call_target="tpu_custom_call" | custom-call | tf_op jit(solution)/shard_map/pallas_call | solution.py:127
  143.8 0.9 copy_bitcast_fusion.1
  144.7 84.1 %all-to-all-done.3.incoming_ref = f32[128,64,128]{2,1,0:T(8,128)} async-done(((f32[128,64,128]{2,1,0:T(8,128)}), f32[128,64,128]{2,1,0:T(8,128)}, u32[]{:S(2)}, u32[]{:S(2)}) %all-to-all-start.3) | async-done | bytes 4194336 | tf_op jit(solution)/shard_map/all_to_all | solution.py:142
  228.8 6.6 %all-to-all-start.2 = ((f32[8,16,8,128]{3,2,1,0:T(8,128)}), f32[8,16,8,128]{3,2,1,0:T(8,128)S(1)}, u32[]{:S(2)}, u32[]{:S(2)}) async-start(f32[8,16,8,128]{3,2,1,0:T(8,128)} %copy_bitcast_fusion.1), calls=%async_computation.2 | async-start | bytes 1048576 | tf_op jit(solution)/shard_map/all_to_all | solution.py:147
  235.5 9.0 %shard_map.48 = f32[16,64,128]{2,1,0:T(8,128)S(1)} custom-call(s32[128]{0:T(128)S(1)} %all_to_all.18.label_ref, f32[128,64,128]{2,1,0:T(8,128)} %all-to-all-done.3.incoming_ref, f32[4,16,128,128]{3,2,1,0:T(8,128)} %right_ref.3), custom_call_target="tpu_custom_call" | custom-call | tf_op jit(solution)/shard_map/pallas_call | solution.py:127
  244.5 0.8 copy_bitcast_fusion
  245.3 1.5 all-to-all-done.2
  246.8 5.7 %all-to-all-start.4 = ((f32[8,16,8,128]{3,2,1,0:T(8,128)}), f32[8,16,8,128]{3,2,1,0:T(8,128)S(1)}, u32[]{:S(2)}, u32[]{:S(2)}) async-start(f32[8,16,8,128]{3,2,1,0:T(8,128)} %copy_bitcast_fusion), calls=%async_computation.4 | async-start | bytes 1048576 | tf_op jit(solution)/shard_map/all_to_all | solution.py:147
  252.5 10.7 %all-to-all-done.4 = f32[8,16,8,128]{3,2,1,0:T(8,128)S(1)} async-done(((f32[8,16,8,128]{3,2,1,0:T(8,128)}), f32[8,16,8,128]{3,2,1,0:T(8,128)S(1)}, u32[]{:S(2)}, u32[]{:S(2)}) %all-to-all-start.4) | async-done | bytes 524320 | tf_op jit(solution)/shard_map/all_to_all | solution.py:147
  263.3 0.7 pad_maximum_fusion
  (7 shorter events, 0.1 us)
Async XLA Ops:
  3.1 20.8 %all-to-all-start = ((s32[32,4,1]{1,2,0:T(1,128)}), s32[32,4,1]{1,2,0:T(1,128)S(1)}, u32[]{:S(2)}, u32[]{:S(2)}) async-start(s32[32,4,1]{1,2,0:T(1,128)} %bitcast.2), calls=%async_computation | async-start | bytes 32768 | tf_op jit(solution)/shard_map/all_to_all | solution.py:138
  11.9 1.2 copy-start.2
  22.0 2.0 copy-start.1
  126.5 102.3 %all-to-all-start.3 = ((f32[128,64,128]{2,1,0:T(8,128)}), f32[128,64,128]{2,1,0:T(8,128)}, u32[]{:S(2)}, u32[]{:S(2)}) async-start(f32[128,64,128]{2,1,0:T(8,128)} %get-tuple-element.8), calls=%async_computation.3 | async-start | bytes 8388608 | tf_op jit(solution)/shard_map/all_to_all | solution.py:142
  134.3 2.2 copy-start
  228.8 17.9 %all-to-all-start.2 = ((f32[8,16,8,128]{3,2,1,0:T(8,128)}), f32[8,16,8,128]{3,2,1,0:T(8,128)S(1)}, u32[]{:S(2)}, u32[]{:S(2)}) async-start(f32[8,16,8,128]{3,2,1,0:T(8,128)} %copy_bitcast_fusion.1), calls=%async_computation.2 | async-start | bytes 1048576 | tf_op jit(solution)/shard_map/all_to_all | solution.py:147
  246.8 16.5 %all-to-all-start.4 = ((f32[8,16,8,128]{3,2,1,0:T(8,128)}), f32[8,16,8,128]{3,2,1,0:T(8,128)S(1)}, u32[]{:S(2)}, u32[]{:S(2)}) async-start(f32[8,16,8,128]{3,2,1,0:T(8,128)} %copy_bitcast_fusion), calls=%async_computation.4 | async-start | bytes 1048576 | tf_op jit(solution)/shard_map/all_to_all | solution.py:147

commit v4 on v3

--- a/solution.py
+++ b/solution.py
@@ -46,7 +46,7 @@
     return item_of_slot.astype(jnp.int32), labels
 
 
-def sender_kernel(item_ref, label_ref, left_ref, psi_ref, *out_refs, term_count):
+def sender_kernel(item_ref, label_ref, left_ref, psi_ref, out_ref, *, term_count, half):
     sector_count = psi_ref.shape[0]
     width = psi_ref.shape[-1]
     band = width // term_count
@@ -57,19 +57,18 @@
         item = item_ref[slot]
         term = item // sector_count
         source = item % sector_count
-        value = split_dot(left_ref[term, source], psi_ref[source])
-        value = jnp.where(label_ref[slot] > 0, value, 0.0)
-        for h, out_ref in enumerate(out_refs):
-            for i in range(term_count):
-                out_ref[j, pl.ds(i * piece, piece), :] = value[
-                    i * band + h * piece:i * band + (h + 1) * piece, :
-                ]
+        rows = jnp.concatenate(
+            [left_ref[term, source, pl.ds(i * band + half * piece, piece), :] for i in range(term_count)],
+            axis=0,
+        )
+        value = split_dot(rows, psi_ref[source])
+        out_ref[j] = jnp.where(label_ref[slot] > 0, value, 0.0)
 
 
-def send_blocks(item_of_slot, labels, left_env, psi, term_count):
+def send_blocks(item_of_slot, labels, left_env, psi, term_count, half):
     slot_count = item_of_slot.shape[0]
     width = psi.shape[-1]
-    half = width // SPLIT
+    rows = width // SPLIT
     grid_spec = pltpu.PrefetchScalarGridSpec(
         num_scalar_prefetch=2,
         grid=(slot_count // GROUP,),
@@ -77,16 +76,12 @@
             pl.BlockSpec(left_env.shape, lambda g, *_: (0, 0, 0, 0)),
             pl.BlockSpec(psi.shape, lambda g, *_: (0, 0, 0)),
         ],
-        out_specs=[
-            pl.BlockSpec((GROUP, half, width), lambda g, *_: (g, 0, 0)) for _ in range(SPLIT)
-        ],
+        out_specs=pl.BlockSpec((GROUP, rows, width), lambda g, *_: (g, 0, 0)),
     )
     return pl.pallas_call(
-        functools.partial(sender_kernel, term_count=term_count),
+        functools.partial(sender_kernel, term_count=term_count, half=half),
         grid_spec=grid_spec,
-        out_shape=[
-            jax.ShapeDtypeStruct((slot_count, half, width), jnp.float32) for _ in range(SPLIT)
-        ],
+        out_shape=jax.ShapeDtypeStruct((slot_count, rows, width), jnp.float32),
         compiler_params=pltpu.CompilerParams(vmem_limit_bytes=48 * 1024 * 1024),
     )(item_of_slot, labels, left_env, psi)
 
@@ -132,13 +127,24 @@
     )(labels, incoming, right_env)
 
 
+def incoming_labels(target):
+    term_count, sector_count = target.shape
+    device_count = lax.axis_size("sector")
+    everyone = lax.all_gather(target, "sector", axis=1, tiled=True)
+    everyone = everyone.reshape(term_count, device_count, sector_count).transpose(1, 0, 2)
+    unused, labels_all = jax.vmap(slot_tables)(everyone)
+    mine = lax.axis_index("sector")
+    labels_in = lax.dynamic_slice_in_dim(labels_all, mine * CAP, CAP, axis=1)
+    return labels_in.reshape(device_count * CAP)
+
+
 def on_device(psi, left_env, right_env, target):
     term_count = lax.axis_size("term")
     item_of_slot, labels = slot_tables(target)
-    labels_in = lax.all_to_all(labels, "sector", split_axis=0, concat_axis=0, tiled=True)
-    outgoing = send_blocks(item_of_slot, labels, left_env, psi, term_count)
+    labels_in = incoming_labels(target)
     results = []
-    for piece_out in outgoing:
+    for half in range(SPLIT):
+        piece_out = send_blocks(item_of_slot, labels, left_env, psi, term_count, half)
         incoming = lax.all_to_all(piece_out, "sector", split_axis=0, concat_axis=0, tiled=True)
         partial_value = receive_blocks(labels_in, incoming, right_env)
         sector_count, rows, width = partial_value.shape

time: 265 us -> 320 us (1.21); the launches traced: 264 us -> 315 us
  local copies, waits for them, and re-layouts: 10.4 us -> 35.9 us
  blocking collectives: 103 us -> 116 us
  Pallas kernels: 25.2 us -> 32.2 us
  waiting for transfers between devices: 96.3 us -> 101 us
    all_gather x0 -> x1, blocking collectives: none -> 116 us  [incoming_labels(): everyone = lax.all_gather(target, 'sector', axis=1, tiled=True)]
    all_to_all x1 -> x0, blocking collectives: 103 us -> none  [on_device(): lax.all_to_all(piece_out, 'sector', split_axis=0, concat_axis=0, tiled=True)]
    gather x1 -> x2, local copies, waits for them, and re-layouts: 1.23 us -> 27.9 us  [slot_tables(): label_of_item[item_of_slot]]
    all_to_all x1 -> x0, starting transfers between devices: 8.75 us -> none  [on_device(): lax.all_to_all(labels, 'sector', split_axis=0, concat_axis=0, tiled=True)]
    all_to_all x1 -> x2, starting transfers between devices: 6.5 us -> 14.8 us  [on_device(): lax.all_to_all(piece_out, 'sector', split_axis=0, concat_axis=0, tiled=True)]
    pallas_call x1 -> x2, Pallas kernels: 8.87 us -> 14.2 us  [send_blocks(): pl.pallas_call(functools.partial(sender_kernel, term_count=term_count, ha...]
    all_to_all x1 -> x2, waiting for transfers between devices: 84.1 us -> 86.9 us  [on_device(): lax.all_to_all(piece_out, 'sector', split_axis=0, concat_axis=0, tiled=True)]
  transfers between devices with their start and end apart: 4 -> 4, of which waited for: 3 -> 3; matrix products, arithmetic and copies ran while one was open for 1% -> 10% of each run, Pallas kernels for 10% -> 8%
where the time goes in v4:
time: 320 us; the launch traced here: 315 us
  blocking collectives  116 us (36%)
  waiting for transfers between devices  101 us (32%)
  local copies, waits for them, and re-layouts  35.9 us (11%)
  Pallas kernels  32.2 us (10%)
  starting transfers between devices  26.4 us (8%)
    all_gather x1, blocking collectives, incoming_labels(): everyone = lax.all_gather(target, 'sector', axis=1, tiled=True)  116 us
    all_to_all x2, waiting for transfers between devices, on_device(): lax.all_to_all(piece_out, 'sector', split_axis=0, concat_axis=0, tiled=True)  86.9 us
    gather x2, local copies, waits for them, and re-layouts, slot_tables(): label_of_item[item_of_slot]  27.9 us
    pallas_call x2, Pallas kernels, receive_blocks(): pl.pallas_call(receiver_kernel, grid_spec=grid_spec, out_shape=jax.ShapeD...  18 us
    all_to_all x2, starting transfers between devices, on_device(): lax.all_to_all(piece_out, 'sector', split_axis=0, concat_axis=0, tiled=True)  14.8 us
    pallas_call x2, Pallas kernels, send_blocks(): pl.pallas_call(functools.partial(sender_kernel, term_count=term_count, ha...  14.2 us
    all_to_all x2, waiting for transfers between devices, on_device(): lax.all_to_all(pieces, 'term', split_axis=0, concat_axis=0, tiled=True)  13.8 us
    all_to_all x2, starting transfers between devices, on_device(): lax.all_to_all(pieces, 'term', split_axis=0, concat_axis=0, tiled=True)  11.6 us
  transfers between devices with their start and end apart: 4, of which 3 were waited for; matrix products, arithmetic and copies ran while one was open for 10% of the time, Pallas kernels for 8%

profile of v4, /device:TPU:96, one launch (start us, length us, event | category | flops | bytes accessed | tf_op | source)
XLA Modules:
  0.0 314.6 jit_solution(13888148486809866746)
XLA Ops:
  0.0 0.8 reshape.211
  0.8 0.2 convert_reduce_fusion.1
  1.0 0.1 select_reduce_fusion.1.item_ref
  1.1 0.1 fusion.1
  1.2 1.2 gather_fusion
  2.4 0.0 copy-start.2
  2.4 1.2 copy-done.2
  3.7 7.1 %shard_map.48 = f32[128,64,128]{2,1,0:T(8,128)S(1)} custom-call(s32[128]{0:T(128)S(1)} %select_reduce_fusion.1.item_ref, s32[128]{0:T(128)S(1)} %broadcast_select_fusion.label_ref, f32[4,16,128,128]{3,2,1,0:T(8,128)} %left_ref.3, f32[16,128,128]{2,1,0:T(8,128)S(1)} %copy-done.2), custom_call_target="tpu_custom_call" | custom-call | tf_op jit(solution)/shard_map/pallas_call | solution.py:81
  10.8 0.0 copy-start.1
  10.8 2.0 copy-done.1
  12.8 0.0 copy-start.3
  12.8 8.9 %all-to-all-start.2 = ((f32[128,64,128]{2,1,0:T(8,128)}), f32[128,64,128]{2,1,0:T(8,128)}, u32[]{:S(2)}, u32[]{:S(2)}) async-start(f32[128,64,128]{2,1,0:T(8,128)} %copy-done.1), calls=%async_computation.2 | async-start | bytes 8388608 | tf_op jit(solution)/shard_map/all_to_all | solution.py:148
  21.7 0.0 copy-done.3
  21.7 7.1 %shard_map.46 = f32[128,64,128]{2,1,0:T(8,128)S(1)} custom-call(s32[128]{0:T(128)S(1)} %select_reduce_fusion.1.item_ref, s32[128]{0:T(128)S(1)} %broadcast_select_fusion.label_ref, f32[4,16,128,128]{3,2,1,0:T(8,128)} %left_ref.3, f32[16,128,128]{2,1,0:T(8,128)S(1)} %copy-done.3), custom_call_target="tpu_custom_call" | custom-call | tf_op jit(solution)/shard_map/pallas_call | solution.py:81
  28.8 0.0 copy-start
  28.9 1.9 copy-done
  30.8 0.0 copy-start.4
  30.8 86.9 %all-to-all-done.2.incoming_ref = f32[128,64,128]{2,1,0:T(8,128)} async-done(((f32[128,64,128]{2,1,0:T(8,128)}), f32[128,64,128]{2,1,0:T(8,128)}, u32[]{:S(2)}, u32[]{:S(2)}) %all-to-all-start.2) | async-done | bytes 4194336 | tf_op jit(solution)/shard_map/all_to_all | solution.py:148
  117.7 5.9 %all-to-all-start = ((f32[128,64,128]{2,1,0:T(8,128)}), f32[128,64,128]{2,1,0:T(8,128)}, u32[]{:S(2)}, u32[]{:S(2)}) async-start(f32[128,64,128]{2,1,0:T(8,128)} %copy-done), calls=%async_computation | async-start | bytes 8388608 | tf_op jit(solution)/shard_map/all_to_all | solution.py:148
  123.5 0.0 copy-done.4
  123.5 116.2 %all-gather = s32[32,16,4]{1,2,0:T(4,128)S(1)} all-gather(s32[1,16,4]{1,2,0:T(4,128)S(1)} %bitcast.31), channel_id=1, replica_groups=mesh['term'=8,'sector'=32] {'sector'}, dimensions={0}, use_global_device_ids=true | all-gather | bytes 8448 | tf_op jit(solution)/shard_map/all_gather | solution.py:133
  239.7 0.1 reshape.229
  239.8 0.1 reshape.208
  239.9 0.1 copy.26
  240.0 0.1 copy.27
  240.1 0.9 convert_reduce_fusion
  241.1 0.4 select_reduce_fusion
  241.5 26.7 %gather_fusion.1 = s32[4096]{0:T(1024)S(1)} fusion(s32[32,64]{1,0:T(8,128)S(1)} %get-tuple-element.6, s32[4096]{0:T(1024)S(1)} %fusion.7), kind=kCustom, calls=%fused_computation.1 | custom fusion | bytes 65536 | tf_op jit(solution)/shard_map/vmap()/gather | solution.py:45
  268.2 0.4 fusion
  268.6 0.1 dynamic-slice_select_fusion
  268.6 0.1 reshape.210.label_ref
  268.7 9.0 %shard_map.49 = f32[16,64,128]{2,1,0:T(8,128)S(1)} custom-call(s32[128]{0:T(128)S(1)} %reshape.210.label_ref, f32[128,64,128]{2,1,0:T(8,128)} %all-to-all-done.2.incoming_ref, f32[4,16,128,128]{3,2,1,0:T(8,128)} %right_ref.3), custom_call_target="tpu_custom_call" | custom-call | tf_op jit(solution)/shard_map/pallas_call | solution.py:122
  277.8 0.9 copy_bitcast_fusion
  278.6 0.0 all-to-all-done.incoming_ref
  278.6 6.6 %all-to-all-start.3 = ((f32[8,16,8,128]{3,2,1,0:T(8,128)}), f32[8,16,8,128]{3,2,1,0:T(8,128)S(1)}, u32[]{:S(2)}, u32[]{:S(2)}) async-start(f32[8,16,8,128]{3,2,1,0:T(8,128)} %copy_bitcast_fusion), calls=%async_computation.3 | async-start | bytes 1048576 | tf_op jit(solution)/shard_map/all_to_all | solution.py:153
  285.3 9.0 %shard_map.47 = f32[16,64,128]{2,1,0:T(8,128)S(1)} custom-call(s32[128]{0:T(128)S(1)} %reshape.210.label_ref, f32[128,64,128]{2,1,0:T(8,128)} %all-to-all-done.incoming_ref, f32[4,16,128,128]{3,2,1,0:T(8,128)} %right_ref.3), custom_call_target="tpu_custom_call" | custom-call | tf_op jit(solution)/shard_map/pallas_call | solution.py:122
  294.3 0.8 copy_bitcast_fusion.1
  295.1 2.3 all-to-all-done.3
  297.4 4.9 %all-to-all-start.1 = ((f32[8,16,8,128]{3,2,1,0:T(8,128)}), f32[8,16,8,128]{3,2,1,0:T(8,128)S(1)}, u32[]{:S(2)}, u32[]{:S(2)}) async-start(f32[8,16,8,128]{3,2,1,0:T(8,128)} %copy_bitcast_fusion.1), calls=%async_computation.1 | async-start | bytes 1048576 | tf_op jit(solution)/shard_map/all_to_all | solution.py:153
  302.4 11.5 %all-to-all-done.1 = f32[8,16,8,128]{3,2,1,0:T(8,128)S(1)} async-done(((f32[8,16,8,128]{3,2,1,0:T(8,128)}), f32[8,16,8,128]{3,2,1,0:T(8,128)S(1)}, u32[]{:S(2)}, u32[]{:S(2)}) %all-to-all-start.1) | async-done | bytes 524320 | tf_op jit(solution)/shard_map/all_to_all | solution.py:153
  313.9 0.7 pad_maximum_fusion
  (13 shorter events, 0.2 us)
Async XLA Ops:
  2.4 1.2 copy-start.2
  10.8 2.0 copy-start.1
  12.8 9.0 %copy-start.3 = (f32[16,128,128]{2,1,0:T(8,128)S(1)}, f32[16,128,128]{2,1,0:T(8,128)}, u32[]{:S(2)}) copy-start(f32[16,128,128]{2,1,0:T(8,128)} %psi_ref.3) | copy-start | bytes 3145732
  12.8 104.9 %all-to-all-start.2 = ((f32[128,64,128]{2,1,0:T(8,128)}), f32[128,64,128]{2,1,0:T(8,128)}, u32[]{:S(2)}, u32[]{:S(2)}) async-start(f32[128,64,128]{2,1,0:T(8,128)} %copy-done.1), calls=%async_computation.2 | async-start | bytes 8388608 | tf_op jit(solution)/shard_map/all_to_all | solution.py:148
  28.8 1.9 copy-start
  30.8 92.8 %copy-start.4 = (s32[4,16]{1,0:T(4,128)S(1)}, s32[4,16]{1,0:T(4,128)}, u32[]{:S(2)}) copy-start(s32[4,16]{1,0:T(4,128)} %param.7) | copy-start | bytes 772
  117.7 161.0 %all-to-all-start = ((f32[128,64,128]{2,1,0:T(8,128)}), f32[128,64,128]{2,1,0:T(8,128)}, u32[]{:S(2)}, u32[]{:S(2)}) async-start(f32[128,64,128]{2,1,0:T(8,128)} %copy-done), calls=%async_computation | async-start | bytes 8388608 | tf_op jit(solution)/shard_map/all_to_all | solution.py:148
  278.6 18.7 %all-to-all-start.3 = ((f32[8,16,8,128]{3,2,1,0:T(8,128)}), f32[8,16,8,128]{3,2,1,0:T(8,128)S(1)}, u32[]{:S(2)}, u32[]{:S(2)}) async-start(f32[8,16,8,128]{3,2,1,0:T(8,128)} %copy_bitcast_fusion), calls=%async_computation.3 | async-start | bytes 1048576 | tf_op jit(solution)/shard_map/all_to_all | solution.py:153
  297.4 16.5 %all-to-all-start.1 = ((f32[8,16,8,128]{3,2,1,0:T(8,128)}), f32[8,16,8,128]{3,2,1,0:T(8,128)S(1)}, u32[]{:S(2)}, u32[]{:S(2)}) async-start(f32[8,16,8,128]{3,2,1,0:T(8,128)} %copy_bitcast_fusion.1), calls=%async_computation.1 | async-start | bytes 1048576 | tf_op jit(solution)/shard_map/all_to_all | solution.py:153
